TPU v7x, 128 devices: a whole 4x4x4 slice. The times are simulated.
128 devices in a mesh: prow: 8 (over x, y_lo), pcol: 16 (over z, y_hi, core).
Axes of the slice: x: 4, y: 4 (y_hi: 2, y_lo: 2; y = y_hi * 2 + y_lo), z: 4, core: 2. Of those that a mesh axis runs over, the one named last changes fastest.
Arguments:
- trailing: bfloat16 [16384, 16384], P('prow', 'pcol'), may hold values from -6 to 6
- lower_slot_blocks: bfloat16 [16, 8192, 128], P('pcol', 'prow'), may hold values from -6 to 6
- l_rows: int32 [16, 64], P(None, 'prow'), may hold values from -1 to 127, as said below
- d_inv: bfloat16 [16, 128, 128], P('pcol'), may hold values from -0.5 to 0.5
- u_panel: bfloat16 [2048, 16384], P('prow', 'pcol'), may hold values from -0.125 to 0.125
- pivot: int32 [16, 128], P('prow'), may hold values from 0 to 127, each once within a row
Outputs:
- schur: bfloat16 [16384, 16384], P('prow', 'pcol')
Inputs may be any that keep to these rules, and one draw needn't show every extreme that they name: `l_rows`: for each panel, the entries are taken in aligned groups of 8, group g belonging to block rows g * 16 to (g + 1) * 16 - 1: the live entries of a group are distinct block rows of that range and come first, followed by -1; a group holds 4 to 8 live entries, and in every panel some group holds exactly 8.
All inputs are finite; a program needn't handle non-finite values.
Results may differ from a plain program's by a relative error of at most 0.0033.
Values may be sent and summed in bfloat16 or wider, within the bound.
No kernel may reach another device: no remote copies, remote signals or barrier semaphores. Data moves between devices by JAX's collectives and lax.ppermute only.
A program may use at most 64 MiB of HBM per device.

v0:
```python
import functools

import jax
import jax.numpy as jnp
from jax import lax
from jax.experimental import pallas as pl
from jax.experimental.pallas import tpu as pltpu
from jax.sharding import PartitionSpec as P


def _update_kernel(u_starts, n_l, rows, table_ref, trailing_ref, *refs):
    n_u = len(u_starts) - 1
    u_hbm = refs[:n_u]
    l_hbm = refs[n_u:n_u + n_l]
    out_ref = refs[n_u + n_l]
    u_scr, l_scr, lrow, sems = refs[n_u + n_l + 1:]
    side = l_scr.shape[-1]
    held = l_scr.shape[0] // n_l
    step = pl.program_id(0)

    u_copies = [
        pltpu.make_async_copy(
            u_hbm[j], u_scr.at[pl.ds(u_starts[j], u_starts[j + 1] - u_starts[j])], sems.at[j]
        )
        for j in range(n_u)
    ]
    l_copies = [
        pltpu.make_async_copy(l_hbm[j], l_scr.at[pl.ds(j * held, held)], sems.at[n_u + j])
        for j in range(n_l)
    ]

    @pl.when(step == 0)
    def _():
        for c in l_copies + u_copies:
            c.start()
        for c in l_copies:
            c.wait()

    groups = rows // side
    panels = lrow.shape[1] // side
    for r in range(groups):
        for p in range(panels):
            idx = table_ref[p, step * groups + r]
            lrow[r * side:(r + 1) * side, p * side:(p + 1) * side] = l_scr[idx]

    @pl.when(step == 0)
    def _():
        for c in u_copies:
            c.wait()

    tile = 256
    for n in range(out_ref.shape[1] // tile):
        cols = slice(n * tile, (n + 1) * tile)
        acc = jnp.dot(lrow[...], u_scr[:, cols], preferred_element_type=jnp.float32)
        out_ref[:, cols] = (trailing_ref[:, cols].astype(jnp.float32) - acc).astype(out_ref.dtype)


def fused_update(table, trailing, u_pieces, l_pieces):
    rows = 256
    side = l_pieces[0].shape[-1]
    held = l_pieces[0].shape[0]
    n_u, n_l = len(u_pieces), len(l_pieces)
    m, n = trailing.shape
    u_starts = [0]
    for piece in u_pieces:
        u_starts.append(u_starts[-1] + piece.shape[0])
    k = u_starts[-1]
    kernel = functools.partial(_update_kernel, tuple(u_starts), n_l, rows)
    any_spec = pl.BlockSpec(memory_space=pl.ANY)
    grid_spec = pltpu.PrefetchScalarGridSpec(
        num_scalar_prefetch=1,
        grid=(m // rows,),
        in_specs=[pl.BlockSpec((rows, n), lambda g, t: (g, 0))] + [any_spec] * (n_u + n_l),
        out_specs=pl.BlockSpec((rows, n), lambda g, t: (g, 0)),
        scratch_shapes=[
            pltpu.VMEM((k, n), u_pieces[0].dtype),
            pltpu.VMEM((n_l * held, side, side), l_pieces[0].dtype),
            pltpu.VMEM((rows, k), l_pieces[0].dtype),
            pltpu.SemaphoreType.DMA((n_u + n_l,)),
        ],
    )
    return pl.pallas_call(
        kernel,
        grid_spec=grid_spec,
        out_shape=jax.ShapeDtypeStruct((m, n), trailing.dtype),
        compiler_params=pltpu.CompilerParams(
            dimension_semantics=("arbitrary",), vmem_limit_bytes=48 * 1024 * 1024
        ),
        cost_estimate=pl.CostEstimate(
            flops=2 * m * k * n, transcendentals=0, bytes_accessed=2 * (2 * m * n + k * n + n_l * held * side * side)
        ),
    )(table, trailing, *u_pieces, *l_pieces)


def per_device(trailing, lower_slot_blocks, l_rows, d_inv, u_panel, pivot):
    side = d_inv.shape[-1]
    row_blocks = trailing.shape[0] // side
    col_count = trailing.shape[1]
    panels, slot_count = l_rows.shape
    n_rows = lax.axis_size("prow")
    u_own = pivot.shape[0]

    fragments = lower_slot_blocks.reshape(-1, slot_count, side, side)
    scaled = jnp.einsum(
        "ksab,kbc->ksac", fragments, d_inv, preferred_element_type=jnp.float32
    ).astype(jnp.bfloat16)
    scaled = jnp.concatenate([scaled, jnp.zeros_like(scaled[:, :1])], axis=1)
    upper_rows = u_panel.reshape(-1, side, col_count)
    lanes = jnp.arange(side, dtype=jnp.int32)
    permuting = (pivot[:, :, None] == lanes[None, None, :]).astype(jnp.bfloat16)
    pivoted = jnp.einsum(
        "kpq,kqn->kpn", permuting, upper_rows, preferred_element_type=jnp.float32
    ).astype(jnp.bfloat16).reshape(-1, col_count)
    me = lax.axis_index("prow")
    x_step = 2

    def shifted(piece, by):
        return lax.ppermute(piece, "prow", [(i, (i + by) % n_rows) for i in range(n_rows)])

    crossed_u = lax.ppermute(pivoted, "prow", [(i, i ^ 1) for i in range(n_rows)])
    pieces = []
    panel_list = []
    for base, flip in ((pivoted, 0), (crossed_u, 1)):
        right = shifted(base, x_step)
        left = shifted(base, -x_step)
        far = shifted(right, x_step) if flip == 0 else shifted(left, -x_step)
        pieces += [base, right, left, far]
        sources = [
            me ^ flip,
            ((me - x_step) % n_rows) ^ flip,
            ((me + x_step) % n_rows) ^ flip,
            ((me + 2 * x_step) % n_rows) ^ flip,
        ]
        for q in sources:
            panel_list += [u_own * q + j for j in range(u_own)]
    order = jnp.stack(panel_list)

    n_cols = lax.axis_size("pcol")
    col = lax.axis_index("pcol")
    z_step = 4
    crossed = lax.ppermute(scaled, "pcol", [(i, i ^ 2) for i in range(n_cols)])
    held = [scaled, crossed]
    for base in (scaled, crossed):
        for hop in range(1, n_cols // z_step):
            held.append(
                lax.ppermute(
                    base, "pcol", [(i, (i + z_step * hop) % n_cols) for i in range(n_cols)]
                )
            )
    swapped = [lax.ppermute(piece, "pcol", [(i, i ^ 1) for i in range(n_cols)]) for piece in held]

    def lower_sources(c):
        hops = [(c - z_step * hop) % n_cols for hop in range(1, n_cols // z_step)]
        return [c, c ^ 2] + hops + [h ^ 2 for h in hops]

    lower_order = jnp.stack(lower_sources(col) + lower_sources(col ^ 1))
    panel_ids = jnp.arange(panels, dtype=jnp.int32)
    lower_pos = jnp.sum(
        jnp.where(lower_order[None, :] == panel_ids[:, None], panel_ids[None, :], 0), axis=1
    )

    local_ids = jnp.where(l_rows >= 0, l_rows - me * row_blocks, -1)
    levels = jnp.arange(row_blocks, dtype=jnp.int32)
    hit = local_ids[:, None, :] == levels[None, :, None]
    present = jnp.any(hit, axis=-1)
    slot_of = jnp.sum(jnp.where(hit, jnp.arange(slot_count, dtype=jnp.int32), 0), axis=-1)
    slot_at = jnp.where(present[order], slot_of[order], slot_count)
    table = lower_pos[order][:, None] * (slot_count + 1) + slot_at
    l_pieces = [piece.reshape(slot_count + 1, side, side) for piece in held + swapped]
    return fused_update(table, trailing, pieces, l_pieces)


def solution(mesh):
    placed = (
        P("prow", "pcol"),
        P("pcol", "prow", None),
        P(None, "prow"),
        P("pcol", None, None),
        P("prow", "pcol"),
        P("prow", None),
    )

    return jax.shard_map(
        per_device, mesh=mesh, in_specs=placed, out_specs=P("prow", "pcol"), check_vma=False
    )
```

profile of v0, /device:TPU:1, one launch (start us, length us, event | category | flops | bytes accessed | tf_op | source)
XLA Modules:
  0.0 94.5 jit_solution(16311596944670123384)
XLA Ops:
  0.0 0.0 copy-start
  0.0 1.2 %fusion = bf16[1,8,128,128]{3,2,1,0:T(8,128)(2,1)S(1)} fusion(bf16[8,128,128]{2,1,0:T(8,128)(2,1)} %bitcast.72, bf16[1,128,128]{2,1,0:T(8,128)(2,1)} %param.9), kind=kOutput, calls=%fused_computation.5 | convolution fusion | flops 33685504 | bytes 557056 | tf_op jit(solution)/shard_map/ksab,kbc->ksac/dot_general | solution.py:104
  1.2 0.8 fusion.5
  2.1 4.6 %collective-permute-start.10 = (bf16[1,9,128,128]{3,2,1,0:T(8,128)(2,1)}, bf16[1,9,128,128]{3,2,1,0:T(8,128)(2,1)S(1)}, u32[]{:S(2)}, u32[]{:S(2)}) collective-permute-start(bf16[1,9,128,128]{3,2,1,0:T(8,128)(2,1)} %get-tuple-element.5), channel_id=1, source_target_pairs={{0,12},{1,13},{2,14},{3,15},{4,0},{5,1},{6,2},{7,3},{8,4},{9,5},{1... | collective-permute-start | bytes 884744 | tf_op jit(solution)/shard_map/ppermute | solution.py:146
  6.6 0.0 collective-permute-start.9
  6.6 0.7 collective-permute-start.8
  7.3 0.0 copy-done
  7.3 1.0 %convolution_convert_fusion = bf16[2,128,1024]{2,1,0:T(8,128)(2,1)S(1)} fusion(bf16[2,128,1024]{2,1,0:T(8,128)(2,1)S(1)} %bitcast.62, s32[2,128]{1,0:T(2,128)} %param.11), kind=kOutput, calls=%fused_computation.3 | convolution fusion | flops 67403776 | bytes 1049600 | tf_op jit(solution)/shard_map/kpq,kqn->kpn/dot_general | solution.py:111
  8.4 1.4 %collective-permute-start.3 = (bf16[256,1024]{1,0:T(8,128)(2,1)S(1)}, bf16[256,1024]{1,0:T(8,128)(2,1)}, u32[]{:S(2)}, u32[]{:S(2)}) collective-permute-start(bf16[256,1024]{1,0:T(8,128)(2,1)S(1)} %bitcast.63), channel_id=1, source_target_pairs={{0,16},{16,0},{32,48},{48,32},{64,80},{80,64},{96,112},{112,96},{1... | collective-permute-start | bytes 1572872 | tf_op jit(solution)/shard_map/ppermute | solution.py:120
  9.7 2.5 %collective-permute-start.1 = (bf16[256,1024]{1,0:T(8,128)(2,1)S(1)}, bf16[256,1024]{1,0:T(8,128)(2,1)}, u32[]{:S(2)}, u32[]{:S(2)}) collective-permute-start(bf16[256,1024]{1,0:T(8,128)(2,1)S(1)} %bitcast.64), channel_id=1, source_target_pairs={{0,96},{16,112},{32,0},{48,16},{64,32},{80,48},{96,64},{112,80},{1... | collective-permute-start | bytes 1572872 | tf_op jit(solution)/shard_map/ppermute | solution.py:118
  12.2 6.6 %collective-permute-done.10 = bf16[1,9,128,128]{3,2,1,0:T(8,128)(2,1)S(1)} collective-permute-done((bf16[1,9,128,128]{3,2,1,0:T(8,128)(2,1)}, bf16[1,9,128,128]{3,2,1,0:T(8,128)(2,1)S(1)}, u32[]{:S(2)}, u32[]{:S(2)}) %collective-permute-start.10) | collective-permute-done | bytes 294944 | tf_op jit(solution)/shard_map/ppermute | solution.py:146
  18.8 1.2 %collective-permute-start = (bf16[256,1024]{1,0:T(8,128)(2,1)S(1)}, bf16[256,1024]{1,0:T(8,128)(2,1)S(1)}, u32[]{:S(2)}, u32[]{:S(2)}) collective-permute-start(bf16[256,1024]{1,0:T(8,128)(2,1)S(1)} %bitcast.65), channel_id=1, source_target_pairs={{0,32},{16,48},{32,64},{48,80},{64,96},{80,112},{96,0},{112,16},{1... | collective-permute-start | bytes 1572872 | tf_op jit(solution)/shard_map/ppermute | solution.py:118
  20.0 0.0 collective-permute-done.9
  20.0 2.9 %collective-permute-start.7 = (bf16[1,9,128,128]{3,2,1,0:T(8,128)(2,1)}, bf16[1,9,128,128]{3,2,1,0:T(8,128)(2,1)S(1)}, u32[]{:S(2)}, u32[]{:S(2)}) collective-permute-start(bf16[1,9,128,128]{3,2,1,0:T(8,128)(2,1)} %get-tuple-element.5), channel_id=1, source_target_pairs={{0,2},{1,3},{2,0},{3,1},{4,6},{5,7},{6,4},{7,5},{8,10},{9,11},{10,... | collective-permute-start | bytes 884744 | tf_op jit(solution)/shard_map/ppermute | solution.py:141
  23.0 0.1 collective-permute-done.8
  23.0 2.2 %collective-permute-start.14 = (bf16[1,9,128,128]{3,2,1,0:T(8,128)(2,1)}, bf16[1,9,128,128]{3,2,1,0:T(8,128)(2,1)S(1)}, u32[]{:S(2)}, u32[]{:S(2)}) collective-permute-start(bf16[1,9,128,128]{3,2,1,0:T(8,128)(2,1)} %get-tuple-element.5), channel_id=1, source_target_pairs={{0,1},{1,0},{2,3},{3,2},{4,5},{5,4},{6,7},{7,6},{8,9},{9,8},{10,11... | collective-permute-start | bytes 884744 | tf_op jit(solution)/shard_map/ppermute | solution.py:150
  25.2 3.9 %collective-permute-done.7 = bf16[1,9,128,128]{3,2,1,0:T(8,128)(2,1)S(1)} collective-permute-done((bf16[1,9,128,128]{3,2,1,0:T(8,128)(2,1)}, bf16[1,9,128,128]{3,2,1,0:T(8,128)(2,1)S(1)}, u32[]{:S(2)}, u32[]{:S(2)}) %collective-permute-start.7) | collective-permute-done | bytes 294944 | tf_op jit(solution)/shard_map/ppermute | solution.py:141
  29.1 2.4 %collective-permute-start.18 = (bf16[1,9,128,128]{3,2,1,0:T(8,128)(2,1)S(1)}, bf16[1,9,128,128]{3,2,1,0:T(8,128)(2,1)}, u32[]{:S(2)}, u32[]{:S(2)}) collective-permute-start(bf16[1,9,128,128]{3,2,1,0:T(8,128)(2,1)S(1)} %collective-permute-done.10), channel_id=1, source_target_pairs={{0,1},{1,0},{2,3},{3,2},{4,5},{5,4},{6,7},{7,6},{8,9},{9,8},{10,11... | collective-permute-start | bytes 884744 | tf_op jit(solution)/shard_map/ppermute | solution.py:150
  31.6 0.0 collective-permute-done.14
  31.6 0.0 collective-permute-start.17
  31.6 0.7 subtract_select_fusion
  32.2 0.1 stack.135
  32.4 0.0 collective-permute-done.3.refs_4_
  32.4 0.6 collective-permute-start.16
  33.0 0.0 collective-permute-done.1.refs_2_
  33.0 3.1 %collective-permute-start.13 = (bf16[1,9,128,128]{3,2,1,0:T(8,128)(2,1)S(1)}, bf16[1,9,128,128]{3,2,1,0:T(8,128)(2,1)}, u32[]{:S(2)}, u32[]{:S(2)}) collective-permute-start(bf16[1,9,128,128]{3,2,1,0:T(8,128)(2,1)S(1)} %collective-permute-done.7), channel_id=1, source_target_pairs={{0,12},{1,13},{2,14},{3,15},{4,0},{5,1},{6,2},{7,3},{8,4},{9,5},{1... | collective-permute-start | bytes 884744 | tf_op jit(solution)/shard_map/ppermute | solution.py:146
  36.0 0.0 collective-permute-done.refs_1_
  36.0 1.5 %collective-permute-start.5 = (bf16[256,1024]{1,0:T(8,128)(2,1)}, bf16[256,1024]{1,0:T(8,128)(2,1)}, u32[]{:S(2)}, u32[]{:S(2)}) collective-permute-start(bf16[256,1024]{1,0:T(8,128)(2,1)} %collective-permute-done.3.refs_4_), channel_id=1, source_target_pairs={{0,96},{16,112},{32,0},{48,16},{64,32},{80,48},{96,64},{112,80},{1... | collective-permute-start | bytes 1572872 | tf_op jit(solution)/shard_map/ppermute | solution.py:118
  37.5 0.1 copy.9
  37.6 0.1 stack.118
  37.7 0.0 collective-permute-done.18
  37.7 0.7 collective-permute-start.15
  38.4 0.0 collective-permute-done.17
  38.4 1.7 %collective-permute-start.12 = (bf16[1,9,128,128]{3,2,1,0:T(8,128)(2,1)S(1)}, bf16[1,9,128,128]{3,2,1,0:T(8,128)(2,1)}, u32[]{:S(2)}, u32[]{:S(2)}) collective-permute-start(bf16[1,9,128,128]{3,2,1,0:T(8,128)(2,1)S(1)} %collective-permute-done.7), channel_id=1, source_target_pairs={{0,8},{1,9},{2,10},{3,11},{4,12},{5,13},{6,14},{7,15},{8,0},{9,1},... | collective-permute-start | bytes 884744 | tf_op jit(solution)/shard_map/ppermute | solution.py:146
  40.1 0.1 select_reduce_fusion.1
  40.2 0.7 gather_fusion
  40.9 0.0 collective-permute-done.16
  40.9 0.3 collective-permute-start.11
  41.2 7.3 %collective-permute-done.13 = bf16[1,9,128,128]{3,2,1,0:T(8,128)(2,1)} collective-permute-done((bf16[1,9,128,128]{3,2,1,0:T(8,128)(2,1)S(1)}, bf16[1,9,128,128]{3,2,1,0:T(8,128)(2,1)}, u32[]{:S(2)}, u32[]{:S(2)}) %collective-permute-start.13) | collective-permute-done | bytes 294944 | tf_op jit(solution)/shard_map/ppermute | solution.py:146
  48.5 1.1 %collective-permute-start.21 = (bf16[1,9,128,128]{3,2,1,0:T(8,128)(2,1)}, bf16[1,9,128,128]{3,2,1,0:T(8,128)(2,1)}, u32[]{:S(2)}, u32[]{:S(2)}) collective-permute-start(bf16[1,9,128,128]{3,2,1,0:T(8,128)(2,1)} %collective-permute-done.13), channel_id=1, source_target_pairs={{0,1},{1,0},{2,3},{3,2},{4,5},{5,4},{6,7},{7,6},{8,9},{9,8},{10,11... | collective-permute-start | bytes 884744 | tf_op jit(solution)/shard_map/ppermute | solution.py:150
  49.6 0.1 select_reduce_fusion
  49.7 0.6 gather_fusion.2
  50.2 0.0 collective-permute-done.15
  50.2 1.3 %collective-permute-start.4 = (bf16[256,1024]{1,0:T(8,128)(2,1)}, bf16[256,1024]{1,0:T(8,128)(2,1)}, u32[]{:S(2)}, u32[]{:S(2)}) collective-permute-start(bf16[256,1024]{1,0:T(8,128)(2,1)} %collective-permute-done.3.refs_4_), channel_id=1, source_target_pairs={{0,32},{16,48},{32,64},{48,80},{64,96},{80,112},{96,0},{112,16},{1... | collective-permute-start | bytes 1572872 | tf_op jit(solution)/shard_map/ppermute | solution.py:118
  51.5 0.0 collective-permute-done.12
  51.5 1.1 %collective-permute-start.2 = (bf16[256,1024]{1,0:T(8,128)(2,1)S(1)}, bf16[256,1024]{1,0:T(8,128)(2,1)}, u32[]{:S(2)}, u32[]{:S(2)}) collective-permute-start(bf16[256,1024]{1,0:T(8,128)(2,1)S(1)} %collective-permute-done.refs_1_), channel_id=1, source_target_pairs={{0,32},{16,48},{32,64},{48,80},{64,96},{80,112},{96,0},{112,16},{1... | collective-permute-start | bytes 1572872 | tf_op jit(solution)/shard_map/ppermute | solution.py:118
  52.6 0.0 collective-permute-done.5.refs_6_
  52.6 1.6 %collective-permute-start.6 = (bf16[256,1024]{1,0:T(8,128)(2,1)}, bf16[256,1024]{1,0:T(8,128)(2,1)}, u32[]{:S(2)}, u32[]{:S(2)}) collective-permute-start(bf16[256,1024]{1,0:T(8,128)(2,1)} %collective-permute-done.5.refs_6_), channel_id=1, source_target_pairs={{0,96},{16,112},{32,0},{48,16},{64,32},{80,48},{96,64},{112,80},{1... | collective-permute-start | bytes 1572872 | tf_op jit(solution)/shard_map/ppermute | solution.py:118
  54.2 1.1 %collective-permute-done.11 = bf16[1,9,128,128]{3,2,1,0:T(8,128)(2,1)} collective-permute-done((bf16[1,9,128,128]{3,2,1,0:T(8,128)(2,1)S(1)}, bf16[1,9,128,128]{3,2,1,0:T(8,128)(2,1)}, u32[]{:S(2)}, u32[]{:S(2)}) %collective-permute-start.11) | collective-permute-done | bytes 294944 | tf_op jit(solution)/shard_map/ppermute | solution.py:146
  55.3 0.5 collective-permute-start.20
  55.8 0.0 collective-permute-done.21
  55.8 0.0 collective-permute-start.19
  55.8 0.1 fusion.2
  55.9 0.6 gather_fusion.1
  56.5 0.1 select_add_fusion.table_ref
  56.6 0.8 collective-permute-done.20
  57.3 0.4 collective-permute-done.19
  57.7 7.6 %collective-permute-done.4.refs_5_ = bf16[256,1024]{1,0:T(8,128)(2,1)} collective-permute-done((bf16[256,1024]{1,0:T(8,128)(2,1)}, bf16[256,1024]{1,0:T(8,128)(2,1)}, u32[]{:S(2)}, u32[]{:S(2)}) %collective-permute-start.4) | collective-permute-done | bytes 524320 | tf_op jit(solution)/shard_map/ppermute | solution.py:118
  65.3 11.2 %collective-permute-done.2.refs_3_ = bf16[256,1024]{1,0:T(8,128)(2,1)} collective-permute-done((bf16[256,1024]{1,0:T(8,128)(2,1)S(1)}, bf16[256,1024]{1,0:T(8,128)(2,1)}, u32[]{:S(2)}, u32[]{:S(2)}) %collective-permute-start.2) | collective-permute-done | bytes 524320 | tf_op jit(solution)/shard_map/ppermute | solution.py:118
  76.6 0.0 collective-permute-done.6.refs_7_
  76.6 18.0 %shard_map.64 = bf16[2048,1024]{1,0:T(8,128)(2,1)} custom-call(s32[16,16]{1,0:T(8,128)S(1)} %select_add_fusion.table_ref, bf16[2048,1024]{1,0:T(8,128)(2,1)} %trailing_ref.1, bf16[256,1024]{1,0:T(8,128)(2,1)S(1)} %bitcast.66, bf16[256,1024]{1,0:T(8,128)(2,1)S(1)} %collective-permute-done.refs_1_, bf16[256,1024]{1,0:T(8,128)(2,1)} %collective-permute-done.1.refs_2_, ...), custom_call_target="tpu_custom_call" | custom-call | flops 8589934592 | bytes 17301504 | tf_op jit(solution)/shard_map/pallas_call | solution.py:82
  (3 shorter events, 0.0 us)
Async XLA Ops:
  0.0 7.3 %copy-start = (bf16[256,1024]{1,0:T(8,128)(2,1)S(1)}, bf16[256,1024]{1,0:T(8,128)(2,1)}, u32[]{:S(2)}) copy-start(bf16[256,1024]{1,0:T(8,128)(2,1)} %param.10) | copy-start | bytes 1572868
  2.1 16.8 %collective-permute-start.10 = (bf16[1,9,128,128]{3,2,1,0:T(8,128)(2,1)}, bf16[1,9,128,128]{3,2,1,0:T(8,128)(2,1)S(1)}, u32[]{:S(2)}, u32[]{:S(2)}) collective-permute-start(bf16[1,9,128,128]{3,2,1,0:T(8,128)(2,1)} %get-tuple-element.5), channel_id=1, source_target_pairs={{0,12},{1,13},{2,14},{3,15},{4,0},{5,1},{6,2},{7,3},{8,4},{9,5},{1... | collective-permute-start | bytes 884744 | tf_op jit(solution)/shard_map/ppermute | solution.py:146
  6.6 13.4 %collective-permute-start.9 = (bf16[1,9,128,128]{3,2,1,0:T(8,128)(2,1)}, bf16[1,9,128,128]{3,2,1,0:T(8,128)(2,1)S(1)}, u32[]{:S(2)}, u32[]{:S(2)}) collective-permute-start(bf16[1,9,128,128]{3,2,1,0:T(8,128)(2,1)} %get-tuple-element.5), channel_id=1, source_target_pairs={{0,8},{1,9},{2,10},{3,11},{4,12},{5,13},{6,14},{7,15},{8,0},{9,1},... | collective-permute-start | bytes 884744 | tf_op jit(solution)/shard_map/ppermute | solution.py:146
  6.6 16.4 %collective-permute-start.8 = (bf16[1,9,128,128]{3,2,1,0:T(8,128)(2,1)}, bf16[1,9,128,128]{3,2,1,0:T(8,128)(2,1)S(1)}, u32[]{:S(2)}, u32[]{:S(2)}) collective-permute-start(bf16[1,9,128,128]{3,2,1,0:T(8,128)(2,1)} %get-tuple-element.5), channel_id=1, source_target_pairs={{0,4},{1,5},{2,6},{3,7},{4,8},{5,9},{6,10},{7,11},{8,12},{9,13},{1... | collective-permute-start | bytes 884744 | tf_op jit(solution)/shard_map/ppermute | solution.py:146
  8.4 24.0 %collective-permute-start.3 = (bf16[256,1024]{1,0:T(8,128)(2,1)S(1)}, bf16[256,1024]{1,0:T(8,128)(2,1)}, u32[]{:S(2)}, u32[]{:S(2)}) collective-permute-start(bf16[256,1024]{1,0:T(8,128)(2,1)S(1)} %bitcast.63), channel_id=1, source_target_pairs={{0,16},{16,0},{32,48},{48,32},{64,80},{80,64},{96,112},{112,96},{1... | collective-permute-start | bytes 1572872 | tf_op jit(solution)/shard_map/ppermute | solution.py:120
  9.7 23.2 %collective-permute-start.1 = (bf16[256,1024]{1,0:T(8,128)(2,1)S(1)}, bf16[256,1024]{1,0:T(8,128)(2,1)}, u32[]{:S(2)}, u32[]{:S(2)}) collective-permute-start(bf16[256,1024]{1,0:T(8,128)(2,1)S(1)} %bitcast.64), channel_id=1, source_target_pairs={{0,96},{16,112},{32,0},{48,16},{64,32},{80,48},{96,64},{112,80},{1... | collective-permute-start | bytes 1572872 | tf_op jit(solution)/shard_map/ppermute | solution.py:118
  18.8 17.2 %collective-permute-start = (bf16[256,1024]{1,0:T(8,128)(2,1)S(1)}, bf16[256,1024]{1,0:T(8,128)(2,1)S(1)}, u32[]{:S(2)}, u32[]{:S(2)}) collective-permute-start(bf16[256,1024]{1,0:T(8,128)(2,1)S(1)} %bitcast.65), channel_id=1, source_target_pairs={{0,32},{16,48},{32,64},{48,80},{64,96},{80,112},{96,0},{112,16},{1... | collective-permute-start | bytes 1572872 | tf_op jit(solution)/shard_map/ppermute | solution.py:118
  20.0 9.1 %collective-permute-start.7 = (bf16[1,9,128,128]{3,2,1,0:T(8,128)(2,1)}, bf16[1,9,128,128]{3,2,1,0:T(8,128)(2,1)S(1)}, u32[]{:S(2)}, u32[]{:S(2)}) collective-permute-start(bf16[1,9,128,128]{3,2,1,0:T(8,128)(2,1)} %get-tuple-element.5), channel_id=1, source_target_pairs={{0,2},{1,3},{2,0},{3,1},{4,6},{5,7},{6,4},{7,5},{8,10},{9,11},{10,... | collective-permute-start | bytes 884744 | tf_op jit(solution)/shard_map/ppermute | solution.py:141
  23.0 8.5 %collective-permute-start.14 = (bf16[1,9,128,128]{3,2,1,0:T(8,128)(2,1)}, bf16[1,9,128,128]{3,2,1,0:T(8,128)(2,1)S(1)}, u32[]{:S(2)}, u32[]{:S(2)}) collective-permute-start(bf16[1,9,128,128]{3,2,1,0:T(8,128)(2,1)} %get-tuple-element.5), channel_id=1, source_target_pairs={{0,1},{1,0},{2,3},{3,2},{4,5},{5,4},{6,7},{7,6},{8,9},{9,8},{10,11... | collective-permute-start | bytes 884744 | tf_op jit(solution)/shard_map/ppermute | solution.py:150
  29.1 8.6 %collective-permute-start.18 = (bf16[1,9,128,128]{3,2,1,0:T(8,128)(2,1)S(1)}, bf16[1,9,128,128]{3,2,1,0:T(8,128)(2,1)}, u32[]{:S(2)}, u32[]{:S(2)}) collective-permute-start(bf16[1,9,128,128]{3,2,1,0:T(8,128)(2,1)S(1)} %collective-permute-done.10), channel_id=1, source_target_pairs={{0,1},{1,0},{2,3},{3,2},{4,5},{5,4},{6,7},{7,6},{8,9},{9,8},{10,11... | collective-permute-start | bytes 884744 | tf_op jit(solution)/shard_map/ppermute | solution.py:150
  31.6 6.9 %collective-permute-start.17 = (bf16[1,9,128,128]{3,2,1,0:T(8,128)(2,1)S(1)}, bf16[1,9,128,128]{3,2,1,0:T(8,128)(2,1)}, u32[]{:S(2)}, u32[]{:S(2)}) collective-permute-start(bf16[1,9,128,128]{3,2,1,0:T(8,128)(2,1)S(1)} %collective-permute-done.9), channel_id=1, source_target_pairs={{0,1},{1,0},{2,3},{3,2},{4,5},{5,4},{6,7},{7,6},{8,9},{9,8},{10,11... | collective-permute-start | bytes 884744 | tf_op jit(solution)/shard_map/ppermute | solution.py:150
  32.4 8.5 %collective-permute-start.16 = (bf16[1,9,128,128]{3,2,1,0:T(8,128)(2,1)S(1)}, bf16[1,9,128,128]{3,2,1,0:T(8,128)(2,1)}, u32[]{:S(2)}, u32[]{:S(2)}) collective-permute-start(bf16[1,9,128,128]{3,2,1,0:T(8,128)(2,1)S(1)} %collective-permute-done.8), channel_id=1, source_target_pairs={{0,1},{1,0},{2,3},{3,2},{4,5},{5,4},{6,7},{7,6},{8,9},{9,8},{10,11... | collective-permute-start | bytes 884744 | tf_op jit(solution)/shard_map/ppermute | solution.py:150
  33.0 15.5 %collective-permute-start.13 = (bf16[1,9,128,128]{3,2,1,0:T(8,128)(2,1)S(1)}, bf16[1,9,128,128]{3,2,1,0:T(8,128)(2,1)}, u32[]{:S(2)}, u32[]{:S(2)}) collective-permute-start(bf16[1,9,128,128]{3,2,1,0:T(8,128)(2,1)S(1)} %collective-permute-done.7), channel_id=1, source_target_pairs={{0,12},{1,13},{2,14},{3,15},{4,0},{5,1},{6,2},{7,3},{8,4},{9,5},{1... | collective-permute-start | bytes 884744 | tf_op jit(solution)/shard_map/ppermute | solution.py:146
  36.0 16.6 %collective-permute-start.5 = (bf16[256,1024]{1,0:T(8,128)(2,1)}, bf16[256,1024]{1,0:T(8,128)(2,1)}, u32[]{:S(2)}, u32[]{:S(2)}) collective-permute-start(bf16[256,1024]{1,0:T(8,128)(2,1)} %collective-permute-done.3.refs_4_), channel_id=1, source_target_pairs={{0,96},{16,112},{32,0},{48,16},{64,32},{80,48},{96,64},{112,80},{1... | collective-permute-start | bytes 1572872 | tf_op jit(solution)/shard_map/ppermute | solution.py:118
  37.7 12.5 %collective-permute-start.15 = (bf16[1,9,128,128]{3,2,1,0:T(8,128)(2,1)S(1)}, bf16[1,9,128,128]{3,2,1,0:T(8,128)(2,1)}, u32[]{:S(2)}, u32[]{:S(2)}) collective-permute-start(bf16[1,9,128,128]{3,2,1,0:T(8,128)(2,1)S(1)} %collective-permute-done.7), channel_id=1, source_target_pairs={{0,1},{1,0},{2,3},{3,2},{4,5},{5,4},{6,7},{7,6},{8,9},{9,8},{10,11... | collective-permute-start | bytes 884744 | tf_op jit(solution)/shard_map/ppermute | solution.py:150
  38.4 13.1 %collective-permute-start.12 = (bf16[1,9,128,128]{3,2,1,0:T(8,128)(2,1)S(1)}, bf16[1,9,128,128]{3,2,1,0:T(8,128)(2,1)}, u32[]{:S(2)}, u32[]{:S(2)}) collective-permute-start(bf16[1,9,128,128]{3,2,1,0:T(8,128)(2,1)S(1)} %collective-permute-done.7), channel_id=1, source_target_pairs={{0,8},{1,9},{2,10},{3,11},{4,12},{5,13},{6,14},{7,15},{8,0},{9,1},... | collective-permute-start | bytes 884744 | tf_op jit(solution)/shard_map/ppermute | solution.py:146
  40.9 14.4 %collective-permute-start.11 = (bf16[1,9,128,128]{3,2,1,0:T(8,128)(2,1)S(1)}, bf16[1,9,128,128]{3,2,1,0:T(8,128)(2,1)}, u32[]{:S(2)}, u32[]{:S(2)}) collective-permute-start(bf16[1,9,128,128]{3,2,1,0:T(8,128)(2,1)S(1)} %collective-permute-done.7), channel_id=1, source_target_pairs={{0,4},{1,5},{2,6},{3,7},{4,8},{5,9},{6,10},{7,11},{8,12},{9,13},{1... | collective-permute-start | bytes 884744 | tf_op jit(solution)/shard_map/ppermute | solution.py:146
  48.5 7.3 %collective-permute-start.21 = (bf16[1,9,128,128]{3,2,1,0:T(8,128)(2,1)}, bf16[1,9,128,128]{3,2,1,0:T(8,128)(2,1)}, u32[]{:S(2)}, u32[]{:S(2)}) collective-permute-start(bf16[1,9,128,128]{3,2,1,0:T(8,128)(2,1)} %collective-permute-done.13), channel_id=1, source_target_pairs={{0,1},{1,0},{2,3},{3,2},{4,5},{5,4},{6,7},{7,6},{8,9},{9,8},{10,11... | collective-permute-start | bytes 884744 | tf_op jit(solution)/shard_map/ppermute | solution.py:150
  50.2 15.1 %collective-permute-start.4 = (bf16[256,1024]{1,0:T(8,128)(2,1)}, bf16[256,1024]{1,0:T(8,128)(2,1)}, u32[]{:S(2)}, u32[]{:S(2)}) collective-permute-start(bf16[256,1024]{1,0:T(8,128)(2,1)} %collective-permute-done.3.refs_4_), channel_id=1, source_target_pairs={{0,32},{16,48},{32,64},{48,80},{64,96},{80,112},{96,0},{112,16},{1... | collective-permute-start | bytes 1572872 | tf_op jit(solution)/shard_map/ppermute | solution.py:118
  51.5 25.0 %collective-permute-start.2 = (bf16[256,1024]{1,0:T(8,128)(2,1)S(1)}, bf16[256,1024]{1,0:T(8,128)(2,1)}, u32[]{:S(2)}, u32[]{:S(2)}) collective-permute-start(bf16[256,1024]{1,0:T(8,128)(2,1)S(1)} %collective-permute-done.refs_1_), channel_id=1, source_target_pairs={{0,32},{16,48},{32,64},{48,80},{64,96},{80,112},{96,0},{112,16},{1... | collective-permute-start | bytes 1572872 | tf_op jit(solution)/shard_map/ppermute | solution.py:118
  52.6 24.0 %collective-permute-start.6 = (bf16[256,1024]{1,0:T(8,128)(2,1)}, bf16[256,1024]{1,0:T(8,128)(2,1)}, u32[]{:S(2)}, u32[]{:S(2)}) collective-permute-start(bf16[256,1024]{1,0:T(8,128)(2,1)} %collective-permute-done.5.refs_6_), channel_id=1, source_target_pairs={{0,96},{16,112},{32,0},{48,16},{64,32},{80,48},{96,64},{112,80},{1... | collective-permute-start | bytes 1572872 | tf_op jit(solution)/shard_map/ppermute | solution.py:118
  55.3 2.0 %collective-permute-start.20 = (bf16[1,9,128,128]{3,2,1,0:T(8,128)(2,1)}, bf16[1,9,128,128]{3,2,1,0:T(8,128)(2,1)}, u32[]{:S(2)}, u32[]{:S(2)}) collective-permute-start(bf16[1,9,128,128]{3,2,1,0:T(8,128)(2,1)} %collective-permute-done.12), channel_id=1, source_target_pairs={{0,1},{1,0},{2,3},{3,2},{4,5},{5,4},{6,7},{7,6},{8,9},{9,8},{10,11... | collective-permute-start | bytes 884744 | tf_op jit(solution)/shard_map/ppermute | solution.py:150
  55.8 2.0 %collective-permute-start.19 = (bf16[1,9,128,128]{3,2,1,0:T(8,128)(2,1)}, bf16[1,9,128,128]{3,2,1,0:T(8,128)(2,1)}, u32[]{:S(2)}, u32[]{:S(2)}) collective-permute-start(bf16[1,9,128,128]{3,2,1,0:T(8,128)(2,1)} %collective-permute-done.11), channel_id=1, source_target_pairs={{0,1},{1,0},{2,3},{3,2},{4,5},{5,4},{6,7},{7,6},{8,9},{9,8},{10,11... | collective-permute-start | bytes 884744 | tf_op jit(solution)/shard_map/ppermute | solution.py:150
where the time goes:
time: 94.7 us; the launch traced here: 94.5 us
  waiting for transfers between devices  39 us (41%)
  starting transfers between devices  31.2 us (33%)
  Pallas kernels  18 us (19%)
  local copies, waits for them, and re-layouts  2.91 us (3%)
  matrix products  2.23 us (2%)
  other arithmetic  1.08 us (1%)
    ppermute x6, waiting for transfers between devices, shifted(): lax.ppermute(piece, 'prow', [(i, (i + by) % n_rows) for i in range(n_rows)])  18.8 us
    pallas_call x1, Pallas kernels, fused_update(): pl.pallas_call(kernel, grid_spec=grid_spec, out_shape=jax.ShapeDtypeStruc...  18 us
    ppermute x6, waiting for transfers between devices, per_device(): lax.ppermute(base, 'pcol', [(i, (i + z_step * hop) % n_cols) for i in ran...  15.1 us
    ppermute x6, starting transfers between devices, per_device(): lax.ppermute(base, 'pcol', [(i, (i + z_step * hop) % n_cols) for i in ran...  10.3 us
    ppermute x6, starting transfers between devices, shifted(): lax.ppermute(piece, 'prow', [(i, (i + by) % n_rows) for i in range(n_rows)])  9.11 us
    ppermute x8, starting transfers between devices, per_device(): lax.ppermute(piece, 'pcol', [(i, i ^ 1) for i in range(n_cols)])  7.52 us
    ppermute x1, waiting for transfers between devices, per_device(): crossed = lax.ppermute(scaled, 'pcol', [(i, i ^ 2) for i in range(n_cols)])  3.93 us
    ppermute x1, starting transfers between devices, per_device(): crossed = lax.ppermute(scaled, 'pcol', [(i, i ^ 2) for i in range(n_cols)])  2.93 us
  transfers between devices with their start and end apart: 22, of which 9 were waited for; matrix products, arithmetic and copies ran while one was open for 4% of the time, Pallas kernels for 0%

commit v1 on v0

--- a/solution.py
+++ b/solution.py
@@ -13,50 +13,73 @@
     u_hbm = refs[:n_u]
     l_hbm = refs[n_u:n_u + n_l]
     out_ref = refs[n_u + n_l]
-    u_scr, l_scr, lrow, sems = refs[n_u + n_l + 1:]
+    u_scr, l_scr, lrow, sems, lsems = refs[n_u + n_l + 1:]
     side = l_scr.shape[-1]
     held = l_scr.shape[0] // n_l
     step = pl.program_id(0)
 
-    u_copies = [
-        pltpu.make_async_copy(
-            u_hbm[j], u_scr.at[pl.ds(u_starts[j], u_starts[j + 1] - u_starts[j])], sems.at[j]
-        )
-        for j in range(n_u)
-    ]
-    l_copies = [
-        pltpu.make_async_copy(l_hbm[j], l_scr.at[pl.ds(j * held, held)], sems.at[n_u + j])
-        for j in range(n_l)
-    ]
-
     @pl.when(step == 0)
     def _():
-        for c in l_copies + u_copies:
+        copies = [
+            pltpu.make_async_copy(
+                u_hbm[j],
+                u_scr.at[pl.ds(u_starts[j], u_starts[j + 1] - u_starts[j])],
+                sems.at[j],
+            )
+            for j in range(n_u)
+        ] + [
+            pltpu.make_async_copy(l_hbm[j], l_scr.at[pl.ds(j * held, held)], sems.at[n_u + j])
+            for j in range(n_l)
+        ]
+        for c in copies:
             c.start()
-        for c in l_copies:
+        for c in copies:
             c.wait()
 
     groups = rows // side
-    panels = lrow.shape[1] // side
-    for r in range(groups):
-        for p in range(panels):
-            idx = table_ref[p, step * groups + r]
-            lrow[r * side:(r + 1) * side, p * side:(p + 1) * side] = l_scr[idx]
+    panels = lrow.shape[2] // side
+    steps = pl.num_programs(0)
+
+    def assembly(at, slot):
+        return [
+            pltpu.make_async_copy(
+                l_scr.at[table_ref[p, at * groups + r]],
+                lrow.at[slot, pl.ds(r * side, side), pl.ds(p * side, side)],
+                lsems.at[slot, r * panels + p],
+            )
+            for r in range(groups)
+            for p in range(panels)
+        ]
 
     @pl.when(step == 0)
     def _():
-        for c in u_copies:
+        for c in assembly(0, 0):
+            c.start()
+        for c in assembly(0, 0):
             c.wait()
 
+    nxt = (step + 1) % 2
+
+    @pl.when(step + 1 < steps)
+    def _():
+        for c in assembly(step + 1, nxt):
+            c.start()
+
+    cur = step % 2
     tile = 256
     for n in range(out_ref.shape[1] // tile):
         cols = slice(n * tile, (n + 1) * tile)
-        acc = jnp.dot(lrow[...], u_scr[:, cols], preferred_element_type=jnp.float32)
+        acc = jnp.dot(lrow[cur], u_scr[:, cols], preferred_element_type=jnp.float32)
         out_ref[:, cols] = (trailing_ref[:, cols].astype(jnp.float32) - acc).astype(out_ref.dtype)
 
+    @pl.when(step + 1 < steps)
+    def _():
+        for c in assembly(step + 1, nxt):
+            c.wait()
+
 
 def fused_update(table, trailing, u_pieces, l_pieces):
-    rows = 256
+    rows = 512
     side = l_pieces[0].shape[-1]
     held = l_pieces[0].shape[0]
     n_u, n_l = len(u_pieces), len(l_pieces)
@@ -75,8 +98,9 @@
         scratch_shapes=[
             pltpu.VMEM((k, n), u_pieces[0].dtype),
             pltpu.VMEM((n_l * held, side, side), l_pieces[0].dtype),
-            pltpu.VMEM((rows, k), l_pieces[0].dtype),
+            pltpu.VMEM((2, rows, k), l_pieces[0].dtype),
             pltpu.SemaphoreType.DMA((n_u + n_l,)),
+            pltpu.SemaphoreType.DMA((2, (rows // side) * (k // side))),
         ],
     )
     return pl.pallas_call(

time: 94.7 us -> 96.4 us (1.018)
  Pallas kernels: 18 us -> 19.6 us
    pallas_call x1, Pallas kernels: 18 us -> 19.6 us  [fused_update(): pl.pallas_call(kernel, grid_spec=grid_spec, out_shape=jax.ShapeDtypeStruc...]
where the time goes in v1:
time: 96.4 us; the launch traced here: 96.2 us
  waiting for transfers between devices  39 us (40%)
  starting transfers between devices  31.2 us (32%)
  Pallas kernels  19.6 us (20%)
  local copies, waits for them, and re-layouts  2.91 us (3%)
  matrix products  2.23 us (2%)
  other arithmetic  1.08 us (1%)
    pallas_call x1, Pallas kernels, fused_update(): pl.pallas_call(kernel, grid_spec=grid_spec, out_shape=jax.ShapeDtypeStruc...  19.6 us
    ppermute x6, waiting for transfers between devices, shifted(): lax.ppermute(piece, 'prow', [(i, (i + by) % n_rows) for i in range(n_rows)])  18.8 us
    ppermute x6, waiting for transfers between devices, per_device(): lax.ppermute(base, 'pcol', [(i, (i + z_step * hop) % n_cols) for i in ran...  15.1 us
    ppermute x6, starting transfers between devices, per_device(): lax.ppermute(base, 'pcol', [(i, (i + z_step * hop) % n_cols) for i in ran...  10.3 us
    ppermute x6, starting transfers between devices, shifted(): lax.ppermute(piece, 'prow', [(i, (i + by) % n_rows) for i in range(n_rows)])  9.11 us
    ppermute x8, starting transfers between devices, per_device(): lax.ppermute(piece, 'pcol', [(i, i ^ 1) for i in range(n_cols)])  7.52 us
    ppermute x1, waiting for transfers between devices, per_device(): crossed = lax.ppermute(scaled, 'pcol', [(i, i ^ 2) for i in range(n_cols)])  3.93 us
    ppermute x1, starting transfers between devices, per_device(): crossed = lax.ppermute(scaled, 'pcol', [(i, i ^ 2) for i in range(n_cols)])  2.93 us
  transfers between devices with their start and end apart: 22, of which 9 were waited for; matrix products, arithmetic and copies ran while one was open for 4% of the time, Pallas kernels for 0%

profile of v1, /device:TPU:1, one launch (start us, length us, event | category | flops | bytes accessed | tf_op | source)
XLA Modules:
  0.0 96.2 jit_solution(5852741017751052203)
XLA Ops:
  0.0 0.0 copy-start
  0.0 1.2 %fusion = bf16[1,8,128,128]{3,2,1,0:T(8,128)(2,1)S(1)} fusion(bf16[8,128,128]{2,1,0:T(8,128)(2,1)} %bitcast.72, bf16[1,128,128]{2,1,0:T(8,128)(2,1)} %param.9), kind=kOutput, calls=%fused_computation.5 | convolution fusion | flops 33685504 | bytes 557056 | tf_op jit(solution)/shard_map/ksab,kbc->ksac/dot_general | solution.py:128
  1.2 0.8 fusion.5
  2.1 4.6 %collective-permute-start.10 = (bf16[1,9,128,128]{3,2,1,0:T(8,128)(2,1)}, bf16[1,9,128,128]{3,2,1,0:T(8,128)(2,1)S(1)}, u32[]{:S(2)}, u32[]{:S(2)}) collective-permute-start(bf16[1,9,128,128]{3,2,1,0:T(8,128)(2,1)} %get-tuple-element.5), channel_id=1, source_target_pairs={{0,12},{1,13},{2,14},{3,15},{4,0},{5,1},{6,2},{7,3},{8,4},{9,5},{1... | collective-permute-start | bytes 884744 | tf_op jit(solution)/shard_map/ppermute | solution.py:170
  6.6 0.0 collective-permute-start.9
  6.6 0.7 collective-permute-start.8
  7.3 0.0 copy-done
  7.3 1.0 %convolution_convert_fusion = bf16[2,128,1024]{2,1,0:T(8,128)(2,1)S(1)} fusion(bf16[2,128,1024]{2,1,0:T(8,128)(2,1)S(1)} %bitcast.62, s32[2,128]{1,0:T(2,128)} %param.11), kind=kOutput, calls=%fused_computation.3 | convolution fusion | flops 67403776 | bytes 1049600 | tf_op jit(solution)/shard_map/kpq,kqn->kpn/dot_general | solution.py:135
  8.4 1.4 %collective-permute-start.3 = (bf16[256,1024]{1,0:T(8,128)(2,1)S(1)}, bf16[256,1024]{1,0:T(8,128)(2,1)}, u32[]{:S(2)}, u32[]{:S(2)}) collective-permute-start(bf16[256,1024]{1,0:T(8,128)(2,1)S(1)} %bitcast.63), channel_id=1, source_target_pairs={{0,16},{16,0},{32,48},{48,32},{64,80},{80,64},{96,112},{112,96},{1... | collective-permute-start | bytes 1572872 | tf_op jit(solution)/shard_map/ppermute | solution.py:144
  9.7 2.5 %collective-permute-start.1 = (bf16[256,1024]{1,0:T(8,128)(2,1)S(1)}, bf16[256,1024]{1,0:T(8,128)(2,1)}, u32[]{:S(2)}, u32[]{:S(2)}) collective-permute-start(bf16[256,1024]{1,0:T(8,128)(2,1)S(1)} %bitcast.64), channel_id=1, source_target_pairs={{0,96},{16,112},{32,0},{48,16},{64,32},{80,48},{96,64},{112,80},{1... | collective-permute-start | bytes 1572872 | tf_op jit(solution)/shard_map/ppermute | solution.py:142
  12.2 6.6 %collective-permute-done.10 = bf16[1,9,128,128]{3,2,1,0:T(8,128)(2,1)S(1)} collective-permute-done((bf16[1,9,128,128]{3,2,1,0:T(8,128)(2,1)}, bf16[1,9,128,128]{3,2,1,0:T(8,128)(2,1)S(1)}, u32[]{:S(2)}, u32[]{:S(2)}) %collective-permute-start.10) | collective-permute-done | bytes 294944 | tf_op jit(solution)/shard_map/ppermute | solution.py:170
  18.8 1.2 %collective-permute-start = (bf16[256,1024]{1,0:T(8,128)(2,1)S(1)}, bf16[256,1024]{1,0:T(8,128)(2,1)S(1)}, u32[]{:S(2)}, u32[]{:S(2)}) collective-permute-start(bf16[256,1024]{1,0:T(8,128)(2,1)S(1)} %bitcast.65), channel_id=1, source_target_pairs={{0,32},{16,48},{32,64},{48,80},{64,96},{80,112},{96,0},{112,16},{1... | collective-permute-start | bytes 1572872 | tf_op jit(solution)/shard_map/ppermute | solution.py:142
  20.0 0.0 collective-permute-done.9
  20.0 2.9 %collective-permute-start.7 = (bf16[1,9,128,128]{3,2,1,0:T(8,128)(2,1)}, bf16[1,9,128,128]{3,2,1,0:T(8,128)(2,1)S(1)}, u32[]{:S(2)}, u32[]{:S(2)}) collective-permute-start(bf16[1,9,128,128]{3,2,1,0:T(8,128)(2,1)} %get-tuple-element.5), channel_id=1, source_target_pairs={{0,2},{1,3},{2,0},{3,1},{4,6},{5,7},{6,4},{7,5},{8,10},{9,11},{10,... | collective-permute-start | bytes 884744 | tf_op jit(solution)/shard_map/ppermute | solution.py:165
  23.0 0.1 collective-permute-done.8
  23.0 2.2 %collective-permute-start.14 = (bf16[1,9,128,128]{3,2,1,0:T(8,128)(2,1)}, bf16[1,9,128,128]{3,2,1,0:T(8,128)(2,1)S(1)}, u32[]{:S(2)}, u32[]{:S(2)}) collective-permute-start(bf16[1,9,128,128]{3,2,1,0:T(8,128)(2,1)} %get-tuple-element.5), channel_id=1, source_target_pairs={{0,1},{1,0},{2,3},{3,2},{4,5},{5,4},{6,7},{7,6},{8,9},{9,8},{10,11... | collective-permute-start | bytes 884744 | tf_op jit(solution)/shard_map/ppermute | solution.py:174
  25.2 3.9 %collective-permute-done.7 = bf16[1,9,128,128]{3,2,1,0:T(8,128)(2,1)S(1)} collective-permute-done((bf16[1,9,128,128]{3,2,1,0:T(8,128)(2,1)}, bf16[1,9,128,128]{3,2,1,0:T(8,128)(2,1)S(1)}, u32[]{:S(2)}, u32[]{:S(2)}) %collective-permute-start.7) | collective-permute-done | bytes 294944 | tf_op jit(solution)/shard_map/ppermute | solution.py:165
  29.1 2.4 %collective-permute-start.18 = (bf16[1,9,128,128]{3,2,1,0:T(8,128)(2,1)S(1)}, bf16[1,9,128,128]{3,2,1,0:T(8,128)(2,1)}, u32[]{:S(2)}, u32[]{:S(2)}) collective-permute-start(bf16[1,9,128,128]{3,2,1,0:T(8,128)(2,1)S(1)} %collective-permute-done.10), channel_id=1, source_target_pairs={{0,1},{1,0},{2,3},{3,2},{4,5},{5,4},{6,7},{7,6},{8,9},{9,8},{10,11... | collective-permute-start | bytes 884744 | tf_op jit(solution)/shard_map/ppermute | solution.py:174
  31.6 0.0 collective-permute-done.14
  31.6 0.0 collective-permute-start.17
  31.6 0.7 subtract_select_fusion
  32.2 0.1 stack.135
  32.4 0.0 collective-permute-done.3.refs_4_
  32.4 0.6 collective-permute-start.16
  33.0 0.0 collective-permute-done.1.refs_2_
  33.0 3.1 %collective-permute-start.13 = (bf16[1,9,128,128]{3,2,1,0:T(8,128)(2,1)S(1)}, bf16[1,9,128,128]{3,2,1,0:T(8,128)(2,1)}, u32[]{:S(2)}, u32[]{:S(2)}) collective-permute-start(bf16[1,9,128,128]{3,2,1,0:T(8,128)(2,1)S(1)} %collective-permute-done.7), channel_id=1, source_target_pairs={{0,12},{1,13},{2,14},{3,15},{4,0},{5,1},{6,2},{7,3},{8,4},{9,5},{1... | collective-permute-start | bytes 884744 | tf_op jit(solution)/shard_map/ppermute | solution.py:170
  36.0 0.0 collective-permute-done.refs_1_
  36.0 1.5 %collective-permute-start.5 = (bf16[256,1024]{1,0:T(8,128)(2,1)}, bf16[256,1024]{1,0:T(8,128)(2,1)}, u32[]{:S(2)}, u32[]{:S(2)}) collective-permute-start(bf16[256,1024]{1,0:T(8,128)(2,1)} %collective-permute-done.3.refs_4_), channel_id=1, source_target_pairs={{0,96},{16,112},{32,0},{48,16},{64,32},{80,48},{96,64},{112,80},{1... | collective-permute-start | bytes 1572872 | tf_op jit(solution)/shard_map/ppermute | solution.py:142
  37.5 0.1 copy.9
  37.6 0.1 stack.118
  37.7 0.0 collective-permute-done.18
  37.7 0.7 collective-permute-start.15
  38.4 0.0 collective-permute-done.17
  38.4 1.7 %collective-permute-start.12 = (bf16[1,9,128,128]{3,2,1,0:T(8,128)(2,1)S(1)}, bf16[1,9,128,128]{3,2,1,0:T(8,128)(2,1)}, u32[]{:S(2)}, u32[]{:S(2)}) collective-permute-start(bf16[1,9,128,128]{3,2,1,0:T(8,128)(2,1)S(1)} %collective-permute-done.7), channel_id=1, source_target_pairs={{0,8},{1,9},{2,10},{3,11},{4,12},{5,13},{6,14},{7,15},{8,0},{9,1},... | collective-permute-start | bytes 884744 | tf_op jit(solution)/shard_map/ppermute | solution.py:170
  40.1 0.1 select_reduce_fusion.1
  40.2 0.7 gather_fusion
  40.9 0.0 collective-permute-done.16
  40.9 0.3 collective-permute-start.11
  41.2 7.3 %collective-permute-done.13 = bf16[1,9,128,128]{3,2,1,0:T(8,128)(2,1)} collective-permute-done((bf16[1,9,128,128]{3,2,1,0:T(8,128)(2,1)S(1)}, bf16[1,9,128,128]{3,2,1,0:T(8,128)(2,1)}, u32[]{:S(2)}, u32[]{:S(2)}) %collective-permute-start.13) | collective-permute-done | bytes 294944 | tf_op jit(solution)/shard_map/ppermute | solution.py:170
  48.5 1.1 %collective-permute-start.21 = (bf16[1,9,128,128]{3,2,1,0:T(8,128)(2,1)}, bf16[1,9,128,128]{3,2,1,0:T(8,128)(2,1)}, u32[]{:S(2)}, u32[]{:S(2)}) collective-permute-start(bf16[1,9,128,128]{3,2,1,0:T(8,128)(2,1)} %collective-permute-done.13), channel_id=1, source_target_pairs={{0,1},{1,0},{2,3},{3,2},{4,5},{5,4},{6,7},{7,6},{8,9},{9,8},{10,11... | collective-permute-start | bytes 884744 | tf_op jit(solution)/shard_map/ppermute | solution.py:174
  49.6 0.1 select_reduce_fusion
  49.7 0.6 gather_fusion.2
  50.2 0.0 collective-permute-done.15
  50.2 1.3 %collective-permute-start.4 = (bf16[256,1024]{1,0:T(8,128)(2,1)}, bf16[256,1024]{1,0:T(8,128)(2,1)}, u32[]{:S(2)}, u32[]{:S(2)}) collective-permute-start(bf16[256,1024]{1,0:T(8,128)(2,1)} %collective-permute-done.3.refs_4_), channel_id=1, source_target_pairs={{0,32},{16,48},{32,64},{48,80},{64,96},{80,112},{96,0},{112,16},{1... | collective-permute-start | bytes 1572872 | tf_op jit(solution)/shard_map/ppermute | solution.py:142
  51.5 0.0 collective-permute-done.12
  51.5 1.1 %collective-permute-start.2 = (bf16[256,1024]{1,0:T(8,128)(2,1)S(1)}, bf16[256,1024]{1,0:T(8,128)(2,1)}, u32[]{:S(2)}, u32[]{:S(2)}) collective-permute-start(bf16[256,1024]{1,0:T(8,128)(2,1)S(1)} %collective-permute-done.refs_1_), channel_id=1, source_target_pairs={{0,32},{16,48},{32,64},{48,80},{64,96},{80,112},{96,0},{112,16},{1... | collective-permute-start | bytes 1572872 | tf_op jit(solution)/shard_map/ppermute | solution.py:142
  52.6 0.0 collective-permute-done.5.refs_6_
  52.6 1.6 %collective-permute-start.6 = (bf16[256,1024]{1,0:T(8,128)(2,1)}, bf16[256,1024]{1,0:T(8,128)(2,1)}, u32[]{:S(2)}, u32[]{:S(2)}) collective-permute-start(bf16[256,1024]{1,0:T(8,128)(2,1)} %collective-permute-done.5.refs_6_), channel_id=1, source_target_pairs={{0,96},{16,112},{32,0},{48,16},{64,32},{80,48},{96,64},{112,80},{1... | collective-permute-start | bytes 1572872 | tf_op jit(solution)/shard_map/ppermute | solution.py:142
  54.2 1.1 %collective-permute-done.11 = bf16[1,9,128,128]{3,2,1,0:T(8,128)(2,1)} collective-permute-done((bf16[1,9,128,128]{3,2,1,0:T(8,128)(2,1)S(1)}, bf16[1,9,128,128]{3,2,1,0:T(8,128)(2,1)}, u32[]{:S(2)}, u32[]{:S(2)}) %collective-permute-start.11) | collective-permute-done | bytes 294944 | tf_op jit(solution)/shard_map/ppermute | solution.py:170
  55.3 0.5 collective-permute-start.20
  55.8 0.0 collective-permute-done.21
  55.8 0.0 collective-permute-start.19
  55.8 0.1 fusion.2
  55.9 0.6 gather_fusion.1
  56.5 0.1 select_add_fusion.table_ref
  56.6 0.8 collective-permute-done.20
  57.3 0.4 collective-permute-done.19
  57.7 7.6 %collective-permute-done.4.refs_5_ = bf16[256,1024]{1,0:T(8,128)(2,1)} collective-permute-done((bf16[256,1024]{1,0:T(8,128)(2,1)}, bf16[256,1024]{1,0:T(8,128)(2,1)}, u32[]{:S(2)}, u32[]{:S(2)}) %collective-permute-start.4) | collective-permute-done | bytes 524320 | tf_op jit(solution)/shard_map/ppermute | solution.py:142
  65.3 11.2 %collective-permute-done.2.refs_3_ = bf16[256,1024]{1,0:T(8,128)(2,1)} collective-permute-done((bf16[256,1024]{1,0:T(8,128)(2,1)S(1)}, bf16[256,1024]{1,0:T(8,128)(2,1)}, u32[]{:S(2)}, u32[]{:S(2)}) %collective-permute-start.2) | collective-permute-done | bytes 524320 | tf_op jit(solution)/shard_map/ppermute | solution.py:142
  76.6 0.0 collective-permute-done.6.refs_7_
  76.6 19.6 %shard_map.64 = bf16[2048,1024]{1,0:T(8,128)(2,1)} custom-call(s32[16,16]{1,0:T(8,128)S(1)} %select_add_fusion.table_ref, bf16[2048,1024]{1,0:T(8,128)(2,1)} %trailing_ref.1, bf16[256,1024]{1,0:T(8,128)(2,1)S(1)} %bitcast.66, bf16[256,1024]{1,0:T(8,128)(2,1)S(1)} %collective-permute-done.refs_1_, bf16[256,1024]{1,0:T(8,128)(2,1)} %collective-permute-done.1.refs_2_, ...), custom_call_target="tpu_custom_call" | custom-call | flops 8589934592 | bytes 17301504 | tf_op jit(solution)/shard_map/pallas_call | solution.py:106
  (3 shorter events, 0.0 us)
Async XLA Ops:
  0.0 7.3 %copy-start = (bf16[256,1024]{1,0:T(8,128)(2,1)S(1)}, bf16[256,1024]{1,0:T(8,128)(2,1)}, u32[]{:S(2)}) copy-start(bf16[256,1024]{1,0:T(8,128)(2,1)} %param.10) | copy-start | bytes 1572868
  2.1 16.8 %collective-permute-start.10 = (bf16[1,9,128,128]{3,2,1,0:T(8,128)(2,1)}, bf16[1,9,128,128]{3,2,1,0:T(8,128)(2,1)S(1)}, u32[]{:S(2)}, u32[]{:S(2)}) collective-permute-start(bf16[1,9,128,128]{3,2,1,0:T(8,128)(2,1)} %get-tuple-element.5), channel_id=1, source_target_pairs={{0,12},{1,13},{2,14},{3,15},{4,0},{5,1},{6,2},{7,3},{8,4},{9,5},{1... | collective-permute-start | bytes 884744 | tf_op jit(solution)/shard_map/ppermute | solution.py:170
  6.6 13.4 %collective-permute-start.9 = (bf16[1,9,128,128]{3,2,1,0:T(8,128)(2,1)}, bf16[1,9,128,128]{3,2,1,0:T(8,128)(2,1)S(1)}, u32[]{:S(2)}, u32[]{:S(2)}) collective-permute-start(bf16[1,9,128,128]{3,2,1,0:T(8,128)(2,1)} %get-tuple-element.5), channel_id=1, source_target_pairs={{0,8},{1,9},{2,10},{3,11},{4,12},{5,13},{6,14},{7,15},{8,0},{9,1},... | collective-permute-start | bytes 884744 | tf_op jit(solution)/shard_map/ppermute | solution.py:170
  6.6 16.4 %collective-permute-start.8 = (bf16[1,9,128,128]{3,2,1,0:T(8,128)(2,1)}, bf16[1,9,128,128]{3,2,1,0:T(8,128)(2,1)S(1)}, u32[]{:S(2)}, u32[]{:S(2)}) collective-permute-start(bf16[1,9,128,128]{3,2,1,0:T(8,128)(2,1)} %get-tuple-element.5), channel_id=1, source_target_pairs={{0,4},{1,5},{2,6},{3,7},{4,8},{5,9},{6,10},{7,11},{8,12},{9,13},{1... | collective-permute-start | bytes 884744 | tf_op jit(solution)/shard_map/ppermute | solution.py:170
  8.4 24.0 %collective-permute-start.3 = (bf16[256,1024]{1,0:T(8,128)(2,1)S(1)}, bf16[256,1024]{1,0:T(8,128)(2,1)}, u32[]{:S(2)}, u32[]{:S(2)}) collective-permute-start(bf16[256,1024]{1,0:T(8,128)(2,1)S(1)} %bitcast.63), channel_id=1, source_target_pairs={{0,16},{16,0},{32,48},{48,32},{64,80},{80,64},{96,112},{112,96},{1... | collective-permute-start | bytes 1572872 | tf_op jit(solution)/shard_map/ppermute | solution.py:144
  9.7 23.2 %collective-permute-start.1 = (bf16[256,1024]{1,0:T(8,128)(2,1)S(1)}, bf16[256,1024]{1,0:T(8,128)(2,1)}, u32[]{:S(2)}, u32[]{:S(2)}) collective-permute-start(bf16[256,1024]{1,0:T(8,128)(2,1)S(1)} %bitcast.64), channel_id=1, source_target_pairs={{0,96},{16,112},{32,0},{48,16},{64,32},{80,48},{96,64},{112,80},{1... | collective-permute-start | bytes 1572872 | tf_op jit(solution)/shard_map/ppermute | solution.py:142
  18.8 17.2 %collective-permute-start = (bf16[256,1024]{1,0:T(8,128)(2,1)S(1)}, bf16[256,1024]{1,0:T(8,128)(2,1)S(1)}, u32[]{:S(2)}, u32[]{:S(2)}) collective-permute-start(bf16[256,1024]{1,0:T(8,128)(2,1)S(1)} %bitcast.65), channel_id=1, source_target_pairs={{0,32},{16,48},{32,64},{48,80},{64,96},{80,112},{96,0},{112,16},{1... | collective-permute-start | bytes 1572872 | tf_op jit(solution)/shard_map/ppermute | solution.py:142
  20.0 9.1 %collective-permute-start.7 = (bf16[1,9,128,128]{3,2,1,0:T(8,128)(2,1)}, bf16[1,9,128,128]{3,2,1,0:T(8,128)(2,1)S(1)}, u32[]{:S(2)}, u32[]{:S(2)}) collective-permute-start(bf16[1,9,128,128]{3,2,1,0:T(8,128)(2,1)} %get-tuple-element.5), channel_id=1, source_target_pairs={{0,2},{1,3},{2,0},{3,1},{4,6},{5,7},{6,4},{7,5},{8,10},{9,11},{10,... | collective-permute-start | bytes 884744 | tf_op jit(solution)/shard_map/ppermute | solution.py:165
  23.0 8.5 %collective-permute-start.14 = (bf16[1,9,128,128]{3,2,1,0:T(8,128)(2,1)}, bf16[1,9,128,128]{3,2,1,0:T(8,128)(2,1)S(1)}, u32[]{:S(2)}, u32[]{:S(2)}) collective-permute-start(bf16[1,9,128,128]{3,2,1,0:T(8,128)(2,1)} %get-tuple-element.5), channel_id=1, source_target_pairs={{0,1},{1,0},{2,3},{3,2},{4,5},{5,4},{6,7},{7,6},{8,9},{9,8},{10,11... | collective-permute-start | bytes 884744 | tf_op jit(solution)/shard_map/ppermute | solution.py:174
  29.1 8.6 %collective-permute-start.18 = (bf16[1,9,128,128]{3,2,1,0:T(8,128)(2,1)S(1)}, bf16[1,9,128,128]{3,2,1,0:T(8,128)(2,1)}, u32[]{:S(2)}, u32[]{:S(2)}) collective-permute-start(bf16[1,9,128,128]{3,2,1,0:T(8,128)(2,1)S(1)} %collective-permute-done.10), channel_id=1, source_target_pairs={{0,1},{1,0},{2,3},{3,2},{4,5},{5,4},{6,7},{7,6},{8,9},{9,8},{10,11... | collective-permute-start | bytes 884744 | tf_op jit(solution)/shard_map/ppermute | solution.py:174
  31.6 6.9 %collective-permute-start.17 = (bf16[1,9,128,128]{3,2,1,0:T(8,128)(2,1)S(1)}, bf16[1,9,128,128]{3,2,1,0:T(8,128)(2,1)}, u32[]{:S(2)}, u32[]{:S(2)}) collective-permute-start(bf16[1,9,128,128]{3,2,1,0:T(8,128)(2,1)S(1)} %collective-permute-done.9), channel_id=1, source_target_pairs={{0,1},{1,0},{2,3},{3,2},{4,5},{5,4},{6,7},{7,6},{8,9},{9,8},{10,11... | collective-permute-start | bytes 884744 | tf_op jit(solution)/shard_map/ppermute | solution.py:174
  32.4 8.5 %collective-permute-start.16 = (bf16[1,9,128,128]{3,2,1,0:T(8,128)(2,1)S(1)}, bf16[1,9,128,128]{3,2,1,0:T(8,128)(2,1)}, u32[]{:S(2)}, u32[]{:S(2)}) collective-permute-start(bf16[1,9,128,128]{3,2,1,0:T(8,128)(2,1)S(1)} %collective-permute-done.8), channel_id=1, source_target_pairs={{0,1},{1,0},{2,3},{3,2},{4,5},{5,4},{6,7},{7,6},{8,9},{9,8},{10,11... | collective-permute-start | bytes 884744 | tf_op jit(solution)/shard_map/ppermute | solution.py:174
  33.0 15.5 %collective-permute-start.13 = (bf16[1,9,128,128]{3,2,1,0:T(8,128)(2,1)S(1)}, bf16[1,9,128,128]{3,2,1,0:T(8,128)(2,1)}, u32[]{:S(2)}, u32[]{:S(2)}) collective-permute-start(bf16[1,9,128,128]{3,2,1,0:T(8,128)(2,1)S(1)} %collective-permute-done.7), channel_id=1, source_target_pairs={{0,12},{1,13},{2,14},{3,15},{4,0},{5,1},{6,2},{7,3},{8,4},{9,5},{1... | collective-permute-start | bytes 884744 | tf_op jit(solution)/shard_map/ppermute | solution.py:170
  36.0 16.6 %collective-permute-start.5 = (bf16[256,1024]{1,0:T(8,128)(2,1)}, bf16[256,1024]{1,0:T(8,128)(2,1)}, u32[]{:S(2)}, u32[]{:S(2)}) collective-permute-start(bf16[256,1024]{1,0:T(8,128)(2,1)} %collective-permute-done.3.refs_4_), channel_id=1, source_target_pairs={{0,96},{16,112},{32,0},{48,16},{64,32},{80,48},{96,64},{112,80},{1... | collective-permute-start | bytes 1572872 | tf_op jit(solution)/shard_map/ppermute | solution.py:142
  37.7 12.5 %collective-permute-start.15 = (bf16[1,9,128,128]{3,2,1,0:T(8,128)(2,1)S(1)}, bf16[1,9,128,128]{3,2,1,0:T(8,128)(2,1)}, u32[]{:S(2)}, u32[]{:S(2)}) collective-permute-start(bf16[1,9,128,128]{3,2,1,0:T(8,128)(2,1)S(1)} %collective-permute-done.7), channel_id=1, source_target_pairs={{0,1},{1,0},{2,3},{3,2},{4,5},{5,4},{6,7},{7,6},{8,9},{9,8},{10,11... | collective-permute-start | bytes 884744 | tf_op jit(solution)/shard_map/ppermute | solution.py:174
  38.4 13.1 %collective-permute-start.12 = (bf16[1,9,128,128]{3,2,1,0:T(8,128)(2,1)S(1)}, bf16[1,9,128,128]{3,2,1,0:T(8,128)(2,1)}, u32[]{:S(2)}, u32[]{:S(2)}) collective-permute-start(bf16[1,9,128,128]{3,2,1,0:T(8,128)(2,1)S(1)} %collective-permute-done.7), channel_id=1, source_target_pairs={{0,8},{1,9},{2,10},{3,11},{4,12},{5,13},{6,14},{7,15},{8,0},{9,1},... | collective-permute-start | bytes 884744 | tf_op jit(solution)/shard_map/ppermute | solution.py:170
  40.9 14.4 %collective-permute-start.11 = (bf16[1,9,128,128]{3,2,1,0:T(8,128)(2,1)S(1)}, bf16[1,9,128,128]{3,2,1,0:T(8,128)(2,1)}, u32[]{:S(2)}, u32[]{:S(2)}) collective-permute-start(bf16[1,9,128,128]{3,2,1,0:T(8,128)(2,1)S(1)} %collective-permute-done.7), channel_id=1, source_target_pairs={{0,4},{1,5},{2,6},{3,7},{4,8},{5,9},{6,10},{7,11},{8,12},{9,13},{1... | collective-permute-start | bytes 884744 | tf_op jit(solution)/shard_map/ppermute | solution.py:170
  48.5 7.3 %collective-permute-start.21 = (bf16[1,9,128,128]{3,2,1,0:T(8,128)(2,1)}, bf16[1,9,128,128]{3,2,1,0:T(8,128)(2,1)}, u32[]{:S(2)}, u32[]{:S(2)}) collective-permute-start(bf16[1,9,128,128]{3,2,1,0:T(8,128)(2,1)} %collective-permute-done.13), channel_id=1, source_target_pairs={{0,1},{1,0},{2,3},{3,2},{4,5},{5,4},{6,7},{7,6},{8,9},{9,8},{10,11... | collective-permute-start | bytes 884744 | tf_op jit(solution)/shard_map/ppermute | solution.py:174
  50.2 15.1 %collective-permute-start.4 = (bf16[256,1024]{1,0:T(8,128)(2,1)}, bf16[256,1024]{1,0:T(8,128)(2,1)}, u32[]{:S(2)}, u32[]{:S(2)}) collective-permute-start(bf16[256,1024]{1,0:T(8,128)(2,1)} %collective-permute-done.3.refs_4_), channel_id=1, source_target_pairs={{0,32},{16,48},{32,64},{48,80},{64,96},{80,112},{96,0},{112,16},{1... | collective-permute-start | bytes 1572872 | tf_op jit(solution)/shard_map/ppermute | solution.py:142
  51.5 25.0 %collective-permute-start.2 = (bf16[256,1024]{1,0:T(8,128)(2,1)S(1)}, bf16[256,1024]{1,0:T(8,128)(2,1)}, u32[]{:S(2)}, u32[]{:S(2)}) collective-permute-start(bf16[256,1024]{1,0:T(8,128)(2,1)S(1)} %collective-permute-done.refs_1_), channel_id=1, source_target_pairs={{0,32},{16,48},{32,64},{48,80},{64,96},{80,112},{96,0},{112,16},{1... | collective-permute-start | bytes 1572872 | tf_op jit(solution)/shard_map/ppermute | solution.py:142
  52.6 24.0 %collective-permute-start.6 = (bf16[256,1024]{1,0:T(8,128)(2,1)}, bf16[256,1024]{1,0:T(8,128)(2,1)}, u32[]{:S(2)}, u32[]{:S(2)}) collective-permute-start(bf16[256,1024]{1,0:T(8,128)(2,1)} %collective-permute-done.5.refs_6_), channel_id=1, source_target_pairs={{0,96},{16,112},{32,0},{48,16},{64,32},{80,48},{96,64},{112,80},{1... | collective-permute-start | bytes 1572872 | tf_op jit(solution)/shard_map/ppermute | solution.py:142
  55.3 2.0 %collective-permute-start.20 = (bf16[1,9,128,128]{3,2,1,0:T(8,128)(2,1)}, bf16[1,9,128,128]{3,2,1,0:T(8,128)(2,1)}, u32[]{:S(2)}, u32[]{:S(2)}) collective-permute-start(bf16[1,9,128,128]{3,2,1,0:T(8,128)(2,1)} %collective-permute-done.12), channel_id=1, source_target_pairs={{0,1},{1,0},{2,3},{3,2},{4,5},{5,4},{6,7},{7,6},{8,9},{9,8},{10,11... | collective-permute-start | bytes 884744 | tf_op jit(solution)/shard_map/ppermute | solution.py:174
  55.8 2.0 %collective-permute-start.19 = (bf16[1,9,128,128]{3,2,1,0:T(8,128)(2,1)}, bf16[1,9,128,128]{3,2,1,0:T(8,128)(2,1)}, u32[]{:S(2)}, u32[]{:S(2)}) collective-permute-start(bf16[1,9,128,128]{3,2,1,0:T(8,128)(2,1)} %collective-permute-done.11), channel_id=1, source_target_pairs={{0,1},{1,0},{2,3},{3,2},{4,5},{5,4},{6,7},{7,6},{8,9},{9,8},{10,11... | collective-permute-start | bytes 884744 | tf_op jit(solution)/shard_map/ppermute | solution.py:174
